TPU v7x, 256 devices: a whole 4x4x8 slice. The times are simulated.
256 devices in a mesh: req: 8 (over z), exp: 8 (over y, core), hid: 4 (over x).
Axes of the slice: x: 4, y: 4, z: 8, core: 2. Of those that a mesh axis runs over, the one named last changes fastest.
Arguments:
- layer_input_rows: bfloat16 [16384, 1536], P(('req', 'exp')), may hold values from -6 to 6
- attention_norm_gain: float32 [1536], replicated
- query_weight: bfloat16 [1536, 1536], P(None, 'hid'), may hold values from -1 to 1
- key_weight: bfloat16 [1536, 512], P(None, 'hid'), may hold values from -1 to 1
- value_weight: bfloat16 [1536, 512], P(None, 'hid'), may hold values from -0.15625 to 0.15625
- attention_output_weight: bfloat16 [1536, 1536], P('hid'), may hold values from -0.15625 to 0.15625
- query_down_factor: bfloat16 [64, 1536, 16], P(('req', 'exp')), may hold values from -0.15625 to 0.15625
- query_up_factor: bfloat16 [64, 16, 1536], P(('req', 'exp')), may hold values from -1.5 to 1.5
- value_down_factor: bfloat16 [64, 1536, 16], P(('req', 'exp')), may hold values from -0.15625 to 0.15625
- value_up_factor: bfloat16 [64, 16, 512], P(('req', 'exp')), may hold values from -1.5 to 1.5
- lengths: int32 [8, 4], P('req'), may hold values from 1 to 1024, 2048 in all within a row
- request_adapter: int32 [8, 4], replicated, may hold values from 0 to 63
- adapter_home_row: int32 [64], replicated, may hold values from 0 to 63, each once
- expert_norm_gain: float32 [1536], replicated, may hold values from 0.4 to 1.6
- routes: int32 [16384, 8], P(('req', 'exp', 'hid')), may hold values from 0 to 39, all different within a row; in each aligned block of 64 rows (0 to 63, 64 to 127, ...) at most 16 rows name the same one
- router_expert_weight: float32 [16384, 8], P(('req', 'exp', 'hid')), may hold values from 0.1 to 0.5
- expert_gate_weight: bfloat16 [40, 1536, 512], P('exp', None, 'hid'), may hold values from -0.15625 to 0.15625
- expert_up_weight: bfloat16 [40, 1536, 512], P('exp', None, 'hid'), may hold values from -0.15625 to 0.15625
- expert_down_weight: bfloat16 [40, 512, 1536], P('exp', 'hid'), may hold values from -0.25 to 0.25
Outputs:
- attn_out: bfloat16 [16384, 1536], P(('req', 'exp', 'hid'))
- expert_out: bfloat16 [16384, 1536], P(('req', 'exp', 'hid'))
Inputs may be any that keep to these rules, and one draw needn't show every extreme that they name: `lengths`: each row sums to 2048; its largest entry is exactly 1024. `adapter_home_row`: each adapter row appears once. `routes`: A row names 8 different experts. In the rows of one device (64 consecutive rows, aligned) no expert is named more than 16 times, a bound that some block reaches in some of them.
All inputs are finite; a program needn't handle non-finite values.
Results may differ from a plain program's by a relative error of at most 0.029.
The roundings to bfloat16 on the way count: a program that leaves them out, or rounds other values in their place, can miss the bound.
Values may be sent and summed in bfloat16 or wider, within the bound.
No kernel may reach another device: no remote copies, remote signals or barrier semaphores. Data moves between devices by JAX's collectives and lax.ppermute only.
A program may use at most 128 MiB of HBM per device.

v0:
```python
import jax
import jax.numpy as jnp
from jax import lax
from jax.sharding import PartitionSpec as P

HEAD_WIDTH = 64
scale_attn = 0.015625
residual_mult = 0.22
norm_eps = 1e-06
rope_base = 10000.0
neg_large = -1e30


def rms_norm(values, norm_gain):
    widened = values.astype(jnp.float32)
    mean_sq = jnp.mean(widened * widened, axis=-1, keepdims=True)
    return (widened * lax.rsqrt(mean_sq + norm_eps) * norm_gain).astype(jnp.bfloat16)


def rotary(heads_in, position):
    half_size = heads_in.shape[-1] // 2
    frequency = rope_base ** (-2.0 * jnp.arange(half_size, dtype=jnp.float32) / heads_in.shape[-1])
    angles = position.astype(jnp.float32)[:, None] * frequency[None, :]
    cosine = jnp.cos(angles)[:, None, :]
    sine_part = jnp.sin(angles)[:, None, :]
    first_half = heads_in[..., :half_size]
    second_half = heads_in[..., half_size:]
    return jnp.concatenate(
        [
            first_half * cosine - second_half * sine_part,
            second_half * cosine + first_half * sine_part,
        ],
        axis=-1,
    )


def request_of(row_ids, group_len):
    request_end = jnp.cumsum(group_len)
    return jnp.sum((row_ids[:, None] >= request_end[None, :]).astype(jnp.int32), axis=1)


def locate(row_ids, group_len):
    request_end = jnp.cumsum(group_len)
    request_start = request_end - group_len
    request = request_of(row_ids, group_len)
    member = request[:, None] == jnp.arange(group_len.shape[0], dtype=jnp.int32)[None, :]
    position = row_ids - jnp.sum(jnp.where(member, request_start[None, :], 0), axis=1)
    return (request, member, position)


def expert_rows(rows_in, expert_gate_weight, expert_up_weight, expert_down_weight):
    gate_act = jnp.einsum(
        "red,edf->ref", rows_in, expert_gate_weight, preferred_element_type=jnp.float32
    )
    upper = jnp.einsum(
        "red,edf->ref", rows_in, expert_up_weight, preferred_element_type=jnp.float32
    )
    hidden = (jax.nn.silu(gate_act) * upper).astype(jnp.bfloat16)
    return jnp.einsum(
        "ref,efd->red", hidden, expert_down_weight, preferred_element_type=jnp.float32
    )


def per_device(
    layer_input_rows,
    attention_norm_gain,
    query_weight,
    key_weight,
    value_weight,
    attention_output_weight,
    query_down_factor,
    query_up_factor,
    value_down_factor,
    value_up_factor,
    lengths,
    request_adapter,
    adapter_home_row,
    expert_norm_gain,
    routes,
    router_expert_weight,
    expert_gate_weight,
    expert_up_weight,
    expert_down_weight,
):
    exp_count = lax.axis_size("exp")
    hid_count = lax.axis_size("hid")
    exp_index = lax.axis_index("exp")
    hid_index = lax.axis_index("hid")
    req_index = lax.axis_index("req")
    query_rows = layer_input_rows.shape[0]
    width = layer_input_rows.shape[1]
    kv_local = key_weight.shape[1] // HEAD_WIDTH
    q_local = query_weight.shape[1] // HEAD_WIDTH
    group_share = q_local // kv_local
    adapter_rank_size = query_down_factor.shape[2]
    requests = lengths.shape[1]
    group_len = lengths[0]
    row_ids = exp_index * query_rows + jnp.arange(query_rows, dtype=jnp.int32)
    request, member, position = locate(row_ids, group_len)
    wanted = lax.dynamic_index_in_dim(request_adapter, req_index, 0, keepdims=False)
    slot_ids = jnp.arange(adapter_home_row.shape[0], dtype=jnp.int32)
    home_of = jnp.sum(
        jnp.where(wanted[:, None] == slot_ids[None, :], adapter_home_row[None, :], 0), axis=1
    )
    pieces = (
        lax.all_gather(query_down_factor, ("req", "exp"), axis=0, tiled=True),
        lax.all_gather(query_up_factor, ("req", "exp"), axis=0, tiled=True),
        lax.all_gather(value_down_factor, ("req", "exp"), axis=0, tiled=True),
        lax.all_gather(value_up_factor, ("req", "exp"), axis=0, tiled=True),
    )
    adapter_bank_rows = jnp.arange(pieces[0].shape[0], dtype=jnp.int32)
    selector = (home_of[:, None] == adapter_bank_rows[None, :]).astype(jnp.bfloat16)
    picked_now = tuple(
        (
            jnp.einsum("jn,nab->jab", selector, piece_in, preferred_element_type=jnp.float32)
            for piece_in in pieces
        )
    )
    chosen = tuple((fresh for fresh in picked_now))
    qa_sel, qb_sel, va_sel, vb_sel = [member_in.astype(jnp.bfloat16) for member_in in chosen]
    normed_rows = rms_norm(layer_input_rows, attention_norm_gain)

    def low_rank_term(a_sel, b_sel, width_cols, offset):
        inner_terms = jnp.einsum(
            "td,jdr->tjr", normed_rows, a_sel, preferred_element_type=jnp.float32
        )
        inner_terms = (
            jnp.where(member[:, :, None], inner_terms, 0.0)
            .reshape(query_rows, requests * adapter_rank_size)
            .astype(jnp.bfloat16)
        )
        right_factor = lax.dynamic_slice_in_dim(b_sel, offset, width_cols, 2).reshape(
            requests * adapter_rank_size, width_cols
        )
        return jnp.dot(inner_terms, right_factor, preferred_element_type=jnp.float32)

    query_cols = q_local * HEAD_WIDTH
    kv_cols = kv_local * HEAD_WIDTH
    query_matrix = jnp.dot(
        normed_rows, query_weight, preferred_element_type=jnp.float32
    ) + low_rank_term(qa_sel, qb_sel, query_cols, hid_index * query_cols)
    query_matrix = rotary(query_matrix.reshape(query_rows, q_local, HEAD_WIDTH), position).astype(
        jnp.bfloat16
    )
    query_matrix = query_matrix.reshape(query_rows, kv_local, group_share, HEAD_WIDTH)
    keys_own = jnp.dot(normed_rows, key_weight, preferred_element_type=jnp.float32)
    keys_own = (
        rotary(keys_own.reshape(query_rows, kv_local, HEAD_WIDTH), position)
        .astype(jnp.bfloat16)
        .reshape(query_rows, kv_cols)
    )
    values_own = jnp.dot(
        normed_rows, value_weight, preferred_element_type=jnp.float32
    ) + low_rank_term(va_sel, vb_sel, kv_cols, hid_index * kv_cols)
    values_own = values_own.astype(jnp.bfloat16)
    running_max = jnp.full((kv_local, group_share, query_rows), neg_large, jnp.float32)
    key_piece = lax.all_gather(keys_own, "exp", axis=0, tiled=True)
    value_piece = lax.all_gather(values_own, "exp", axis=0, tiled=True)
    piece_len = key_piece.shape[0]
    key_ids = jnp.arange(piece_len, dtype=jnp.int32)
    key_request = request_of(key_ids, group_len)
    allowed = (request[:, None] == key_request[None, :]) & (key_ids[None, :] <= row_ids[:, None])
    key_heads = key_piece.reshape(piece_len, kv_local, HEAD_WIDTH)
    value_heads = value_piece.reshape(piece_len, kv_local, HEAD_WIDTH)
    scores = (
        jnp.einsum("qkgh,nkh->kgqn", query_matrix, key_heads, preferred_element_type=jnp.float32)
        * scale_attn
    )
    scores = jnp.where(allowed[None, None], scores, neg_large)
    new_max = jnp.maximum(running_max, jnp.max(scores, axis=-1))
    weights = jnp.where(allowed[None, None], jnp.exp(scores - new_max[..., None]), 0.0)
    running_sum = jnp.sum(weights, axis=-1)
    running_out = jnp.einsum(
        "kgqn,nkh->kgqh",
        weights.astype(jnp.bfloat16),
        value_heads,
        preferred_element_type=jnp.float32,
    )
    running_max, running_sum, running_out = (new_max, running_sum, running_out)
    attended = (running_out / running_sum[..., None]).astype(jnp.bfloat16)
    attended = jnp.transpose(attended, (2, 0, 1, 3)).reshape(query_rows, query_cols)
    tok_rows = query_rows // hid_count
    attn_out = lax.psum_scatter(
        jnp.dot(attended, attention_output_weight, preferred_element_type=jnp.float32).astype(
            jnp.bfloat16
        ),
        "hid",
        scatter_dimension=0,
        tiled=True,
    )
    own_rows = lax.dynamic_slice_in_dim(layer_input_rows, hid_index * tok_rows, tok_rows, 0)
    mixed_rows = own_rows.astype(jnp.float32) + residual_mult * attn_out.astype(jnp.float32)
    normed_moe = rms_norm(mixed_rows, expert_norm_gain)
    local_exp = expert_gate_weight.shape[0]
    expert_count = local_exp * exp_count
    top_count = routes.shape[1]
    capacity = max(2, tok_rows // 4)
    flat_route = routes.reshape(tok_rows * top_count)
    route_hits = (flat_route[:, None] == jnp.arange(expert_count, dtype=jnp.int32)[None, :]).astype(
        jnp.int32
    )
    earlier = jnp.cumsum(route_hits, axis=0) - route_hits
    slot_pos = jnp.sum(earlier * route_hits, axis=1)
    slots = slot_pos * expert_count + flat_route
    slot_table = jnp.arange(capacity * expert_count, dtype=jnp.int32)
    placed = jnp.any(
        slot_table[:, None, None] == slots.reshape(tok_rows, top_count)[None], axis=2
    ).astype(jnp.bfloat16)
    outgoing = jnp.dot(placed, normed_moe, preferred_element_type=jnp.float32).astype(jnp.bfloat16)
    outgoing = outgoing.reshape(capacity, expert_count, width)
    copies = jnp.broadcast_to(
        outgoing.reshape(capacity, exp_count, 1, local_exp, width),
        (capacity, exp_count, hid_count, local_exp, width),
    )
    copies = copies.reshape(capacity, exp_count * hid_count * local_exp, width)
    arrived = lax.all_to_all(copies, ("exp", "hid"), split_axis=1, concat_axis=0, tiled=True)
    partials = expert_rows(
        arrived, expert_gate_weight, expert_up_weight, expert_down_weight
    ).astype(jnp.bfloat16)
    returned = lax.all_to_all(partials, ("exp", "hid"), split_axis=0, concat_axis=1, tiled=True)
    returned = returned.reshape(capacity, exp_count, hid_count, local_exp, width)
    results = jnp.sum(returned.astype(jnp.float32), axis=2).astype(jnp.bfloat16)
    results = results.reshape(capacity * expert_count, width)
    picked = jnp.take(results, slots, axis=0).reshape(tok_rows, top_count, width)
    expert_out = jnp.sum(
        router_expert_weight[:, :, None] * picked.astype(jnp.float32), axis=1
    ).astype(jnp.bfloat16)
    return (attn_out, expert_out)


def solution(mesh):
    in_specs = (
        P(("req", "exp"), None),
        P(),
        P(None, "hid"),
        P(None, "hid"),
        P(None, "hid"),
        P("hid", None),
        P(("req", "exp"), None, None),
        P(("req", "exp"), None, None),
        P(("req", "exp"), None, None),
        P(("req", "exp"), None, None),
        P("req", None),
        P(),
        P(),
        P(),
        P(("req", "exp", "hid"), None),
        P(("req", "exp", "hid"), None),
        P("exp", None, "hid"),
        P("exp", None, "hid"),
        P("exp", "hid", None),
    )
    out_specs = (P(("req", "exp", "hid"), None), P(("req", "exp", "hid"), None))
    return jax.shard_map(
        per_device, mesh=mesh, in_specs=in_specs, out_specs=out_specs, check_vma=False
    )
```

profile of v0, /device:TPU:1, one launch (start us, length us, event | category | flops | bytes accessed | tf_op | source)
XLA Modules:
  0.0 728.0 jit_solution(7659078790844080535)
XLA Ops:
  7.2 0.7 all-gather.11.cloned.1.call-update
  8.0 0.7 all-gather.5.cloned.1.call-update
  8.7 0.7 all-gather.7.cloned.1.call-update
  10.0 0.8 reduce-window.10
  10.9 0.9 dynamic-slice_reduce_fusion
  11.8 0.8 select_reduce_fusion.1
  12.8 0.7 fusion.63
  13.5 1.4 fusion.19
  15.1 1.7 fusion.82
  17.4 17.2 %all_gather.18 = bf16[2048,128]{0,1:T(8,128)(2,1)} all-gather(bf16[256,128]{0,1:T(8,128)(2,1)S(1)} %bitcast.138), channel_id=1, replica_groups=mesh['req'=8,'exp'=8,'hid'=4] {'exp'}, dimensions={0}, use_global_device_ids=true | all-gather | bytes 589824 | tf_op jit(solution)/shard_map/all_gather | solution.py:157
  35.2 56.6 %all-gather.11.cloned.1.call-done = bf16[64,16,512]{2,1,0:T(8,128)(2,1)} async-done(((bf16[1,16,512]{2,1,0:T(8,128)(2,1)}), bf16[64,16,512]{2,1,0:T(8,128)(2,1)}) %all-gather.11.cloned.1.call-update) | async-done | bytes 1048592 | tf_op jit(solution)/shard_map/all_gather | solution.py:109
  91.8 2.4 fusion.34
  94.2 76.1 %all-gather.5.cloned.1.call-done = bf16[64,1536,16]{1,2,0:T(8,128)(2,1)} async-done(((bf16[1,1536,16]{1,2,0:T(8,128)(2,1)}), bf16[64,1536,16]{1,2,0:T(8,128)(2,1)}) %all-gather.5.cloned.1.call-update) | async-done | bytes 3145744 | tf_op jit(solution)/shard_map/all_gather | solution.py:106
  170.3 5.3 fusion.12
  175.6 72.9 %all-gather.7.cloned.1.call-done = bf16[64,16,1536]{2,1,0:T(8,128)(2,1)} async-done(((bf16[1,16,1536]{2,1,0:T(8,128)(2,1)}), bf16[64,16,1536]{2,1,0:T(8,128)(2,1)}) %all-gather.7.cloned.1.call-update) | async-done | bytes 3145744 | tf_op jit(solution)/shard_map/all_gather | solution.py:107
  248.5 5.4 fusion.8
  254.7 1.4 convolution_add_fusion
  256.1 1.9 copy.89
  258.0 1.1 subtract_convert_fusion
  259.1 7.7 %fusion = (f32[2,3,256]{2,1,0:T(4,128)S(1)}, f32[2,2048,256,3]{2,1,3,0:T(8,128)}) fusion(pred[256,2048]{0,1:T(8,128)(4,1)S(1)} %fusion.18, bf16[2048,2,64,1]{0,2,3,1:T(8,128)(2,1)} %bitcast.136, bf16[256,2,3,32]{0,3,2,1:T(8,128)(2,1)S(1)} %bitcast.144, bf16[256,2,3,32]{0,3,2,1:T(8,128)(2,1)S(1)} %bitcast.143), kind=kOutput, calls=%fused_computation.3 | convolution fusion | flops 412482048 | bytes 13834240 | tf_op jit(solution)/shard_map/qkgh,nkh->kgqn/dot_general | solution.py:166
  266.7 0.6 broadcast_maximum_fusion
  267.3 59.3 %all-gather.9.cloned.1.call-done = bf16[64,1536,16]{1,2,0:T(8,128)(2,1)} async-done(((bf16[1,1536,16]{1,2,0:T(8,128)(2,1)}), bf16[64,1536,16]{1,2,0:T(8,128)(2,1)}) %all-gather.9.cloned.1.call-update) | async-done | bytes 3145744 | tf_op jit(solution)/shard_map/all_gather | solution.py:108
  326.6 5.8 fusion.15
  333.6 13.2 %all_gather.23 = bf16[2048,128]{1,0:T(8,128)(2,1)S(1)} all-gather(bf16[256,128]{1,0:T(8,128)(2,1)S(1)} %fusion.33), channel_id=1, replica_groups=mesh['req'=8,'exp'=8,'hid'=4] {'exp'}, dimensions={0}, use_global_device_ids=true | all-gather | bytes 589824 | tf_op jit(solution)/shard_map/all_gather | solution.py:158
  347.0 7.5 %fusion.1 = f32[2,3,256]{2,1,0:T(4,128)S(1)} fusion(f32[2,2048,256,3]{2,1,3,0:T(8,128)} %get-tuple-element.11, f32[2,3,256]{2,1,0:T(4,128)} %broadcast_maximum_fusion, pred[256,2048]{0,1:T(8,128)(4,1)S(1)} %fusion.18), kind=kLoop, calls=%fused_computation.4 | loop fusion | flops 15727104 | bytes 13119488 | tf_op jit(solution)/shard_map/reduce_sum | solution.py:172
  354.5 0.7 copy-done.2
  355.3 3.6 fusion.39
  358.9 1.5 convolution_convert_fusion.1
  360.7 1.2 reduce-window.11
  363.0 17.3 %reduce-scatter.2.cloned.1.call-done = bf16[64,1536]{1,0:T(8,128)(2,1)} async-done(((bf16[256,1536]{1,0:T(8,128)(2,1)}), bf16[64,1536]{1,0:T(8,128)(2,1)}) %reduce-scatter.2.cloned.1.call-update) | async-done | bytes 196624 | tf_op jit(solution)/shard_map/reduce_scatter | solution.py:183
  380.3 1.1 multiply_reduce_fusion.1
  381.5 3.0 convolution_convert_fusion
  384.4 4.3 broadcast_in_dim.129
  388.7 3.2 copy.103
  391.9 1.0 broadcast_in_dim.130
  392.8 98.3 %all_to_all.33 = bf16[16,160,1536]{2,0,1:T(8,128)(2,1)S(1)} all-to-all(bf16[16,160,1536]{2,0,1:T(8,128)(2,1)S(1)} %bitcast.131), channel_id=1, replica_groups=mesh['req'=8,'exp'=8,'hid'=4] {'exp','hid'}, dimensions={1} | all-to-all | bytes 15728640 | tf_op jit(solution)/shard_map/all_to_all | solution.py:216
  491.1 3.9 copy.104
  495.0 6.0 convolution_bitcast_fusion.1
  501.0 12.2 %convert_bitcast_fusion = bf16[512,5,1536]{2,0,1:T(8,128)(2,1)} fusion(bf16[5,128,1536]{2,1,0:T(8,128)(2,1)S(1)} %copy-done, bf16[512,5,1536]{2,0,1:T(8,128)(2,1)} %bitcast.134, bf16[5,1536,128]{2,1,0:T(8,128)(2,1)} %param.36, f32[512,5,128]{2,0,1:T(8,128)S(1)} %convolution_bitcast_fusion.1), kind=kOutput, calls=%fused_computation.6 | convolution fusion | flops 2019164160 | bytes 20971520 | tf_op jit(solution)/shard_map/ref,efd->red/dot_general | solution.py:59
  513.2 12.0 %copy.105 = bf16[512,5,1536]{2,1,0:T(8,128)(2,1)} copy(bf16[512,5,1536]{2,0,1:T(8,128)(2,1)} %convert_bitcast_fusion) | data formatting | bytes 15728640 | tf_op jit(solution)/shard_map/convert_element_type | solution.py:219
  525.1 5.6 all-to-all-start.1
  530.9 0.7 copy.96
  531.6 162.9 %all-to-all-done.1 = bf16[512,5,1536]{2,1,0:T(8,128)(2,1)} async-done(((bf16[512,5,1536]{2,1,0:T(8,128)(2,1)}), bf16[512,5,1536]{2,1,0:T(8,128)(2,1)}, u32[]{:S(2)}, u32[]{:S(2)}) %all-to-all-start.1) | async-done | bytes 7864352 | tf_op jit(solution)/shard_map/all_to_all | solution.py:220
  694.5 10.2 %reduce.1 = bf16[16,8,5,1536]{3,2,0,1:T(8,128)(2,1)} reduce(bf16[16,8,4,5,1536]{4,3,0,2,1:T(8,128)(2,1)} %bitcast.39, bf16[]{:T(256)} %constant.89.clone.1), dimensions={2}, to_apply=%region_14.15 | reduce | flops 2949120 | bytes 9830402 | tf_op jit(solution)/shard_map/reduce_sum | solution.py:222
  704.7 3.9 copy.107
  708.6 4.3 reshape.289
  712.9 5.5 gather_fusion
  718.4 2.8 multiply_reduce_fusion
  (89 shorter events, 6.0 us)
Async XLA Ops:
  7.2 493.8 %copy-start = (bf16[5,128,1536]{2,1,0:T(8,128)(2,1)S(1)}, bf16[5,128,1536]{2,1,0:T(8,128)(2,1)}, u32[]{:S(2)}) copy-start(bf16[5,128,1536]{2,1,0:T(8,128)(2,1)} %param.37) | copy-start | bytes 5898244
  7.2 84.6 %all-gather.11.cloned.1.call-start = ((), (), s32[]{:S(2)}) async-start(), calls=%async_computation.6 | async-start | bytes 1064960 | tf_op jit(solution)/shard_map/all_gather | solution.py:109
  7.9 162.4 %all-gather.5.cloned.1.call-start = ((), (), s32[]{:S(2)}) async-start(), calls=%async_computation.3 | async-start | bytes 3194880 | tf_op jit(solution)/shard_map/all_gather | solution.py:106
  8.7 239.9 %all-gather.7.cloned.1.call-start = ((), (), s32[]{:S(2)}) async-start(), calls=%async_computation.4 | async-start | bytes 3194880 | tf_op jit(solution)/shard_map/all_gather | solution.py:107
  9.4 317.2 %all-gather.9.cloned.1.call-start = ((), (), s32[]{:S(2)}) async-start(), calls=%async_computation.5 | async-start | bytes 3194880 | tf_op jit(solution)/shard_map/all_gather | solution.py:108
  10.0 370.3 %reduce-scatter.2.cloned.1.call-start = ((), (), s32[]{:S(2)}) async-start(), calls=%async_computation.7 | async-start | bytes 983040 | tf_op jit(solution)/shard_map/reduce_scatter | solution.py:183
  12.7 157.6 %copy-start.9 = (s32[4]{0:T(128)}, s32[4]{0:T(128)S(1)}, u32[]{:S(2)}) copy-start(s32[4]{0:T(128)S(1)} %select_reduce_fusion.1) | copy-start | bytes 52
  14.9 20.3 %copy-start.14 = (f32[256]{0:T(256)}, f32[256]{0:T(256)S(1)}, u32[]{:S(2)}) copy-start(f32[256]{0:T(256)S(1)} %add_rsqrt_fusion) | copy-start | bytes 3076
  175.6 78.3 %copy-start.3 = (bf16[256,1536]{1,0:T(8,128)(2,1)S(1)}, bf16[256,1536]{1,0:T(8,128)(2,1)}, u32[]{:S(2)}) copy-start(bf16[256,1536]{1,0:T(8,128)(2,1)} %param.19) | copy-start | bytes 2359300
  248.5 5.4 copy-start.15
  248.5 5.5 copy-start.19
  248.5 5.9 copy-start.11
  248.5 6.1 copy-start.17
  259.0 67.5 %copy-start.10 = (s32[4]{0:T(128)S(1)}, s32[4]{0:T(128)}, u32[]{:S(2)}) copy-start(s32[4]{0:T(128)} %copy-done.9) | copy-start | bytes 52
  266.7 65.7 %copy-start.16 = (f32[256]{0:T(256)S(1)}, f32[256]{0:T(256)}, u32[]{:S(2)}) copy-start(f32[256]{0:T(256)} %copy-done.14) | copy-start | bytes 3076
  266.7 65.7 %copy-start.20 = (f32[1536]{0:T(1024)S(1)}, f32[1536]{0:T(1024)}, u32[]{:S(2)}) copy-start(f32[1536]{0:T(1024)} %param.20) | copy-start | bytes 18436
  267.3 65.6 %copy-start.12 = (pred[256,4]{0,1:T(4,128)(4,1)S(1)}, pred[256,4]{0,1:T(4,128)(4,1)}, u32[]{:S(2)}) copy-start(pred[256,4]{0,1:T(4,128)(4,1)} %iota_compare_fusion.5) | copy-start | bytes 3076
  326.6 6.5 copy-start.18
  347.0 8.2 %copy-start.2 = (f32[2,2048,256,3]{2,1,3,0:T(8,128)S(1)}, f32[2,2048,256,3]{2,1,3,0:T(8,128)}, u32[]{:S(2)}) copy-start(f32[2,2048,256,3]{2,1,3,0:T(8,128)} %get-tuple-element.11) | copy-start | bytes 37748740
  347.0 8.2 %copy-start.6 = (f32[2,3,256]{2,1,0:T(4,128)S(1)}, f32[2,3,256]{2,1,0:T(4,128)}, u32[]{:S(2)}) copy-start(f32[2,3,256]{2,1,0:T(4,128)} %broadcast_maximum_fusion) | copy-start | bytes 18436
  355.2 3.6 copy-start.5
  358.9 1.5 copy-start.7
  358.9 21.5 %copy-start.4 = (bf16[256,1536]{1,0:T(8,128)(2,1)S(1)}, bf16[256,1536]{1,0:T(8,128)(2,1)}, u32[]{:S(2)}) copy-start(bf16[256,1536]{1,0:T(8,128)(2,1)} %param.19) | copy-start | bytes 2359300
  358.9 22.6 %copy-start.8 = (f32[1536]{0:T(1024)S(1)}, f32[1536]{0:T(1024)}, u32[]{:S(2)}) copy-start(f32[1536]{0:T(1024)} %param.32) | copy-start | bytes 18436
  525.1 5.8 copy-start.13
  525.1 169.4 %all-to-all-start.1 = ((bf16[512,5,1536]{2,1,0:T(8,128)(2,1)}), bf16[512,5,1536]{2,1,0:T(8,128)(2,1)}, u32[]{:S(2)}, u32[]{:S(2)}) async-start(bf16[512,5,1536]{2,1,0:T(8,128)(2,1)} %copy.105), calls=%async_computation.2 | async-start | bytes 25165824 | tf_op jit(solution)/shard_map/all_to_all | solution.py:220
  712.9 8.3 %copy-start.1 = (bf16[5,128,1536]{2,1,0:T(8,128)(2,1)S(1)}, bf16[5,128,1536]{2,1,0:T(8,128)(2,1)}, u32[]{:S(2)}) copy-start(bf16[5,128,1536]{2,1,0:T(8,128)(2,1)} %param.37) | copy-start | bytes 5898244
Sparse Core Ops, SparseCore 0:
  10.8 80.9 all-gather.10
  94.6 75.7 all-gather.4
  173.1 75.4 all-gather.6
  251.1 75.4 all-gather.8
  360.5 19.7 reduce-scatter.1
where the time goes:
time: 739 us; the launch traced here: 728 us
  waiting for transfers between devices  448 us (61%)
  blocking collectives  129 us (17%)
  matrix products  57.6 us (8%)
  local copies, waits for them, and re-layouts  43.5 us (6%)
  other arithmetic  30.3 us (4%)
  between operations  14.4 us (2%)
    all_to_all x1, waiting for transfers between devices, per_device(): lax.all_to_all(partials, ('exp', 'hid'), split_axis=0, concat_axis=1, til...  163 us
    all_to_all x1, blocking collectives, per_device(): lax.all_to_all(copies, ('exp', 'hid'), split_axis=1, concat_axis=0, tiled...  98.3 us
    all_gather x1, waiting for transfers between devices, per_device(): lax.all_gather(query_down_factor, ('req', 'exp'), axis=0, tiled=True)  76.1 us
    all_gather x1, waiting for transfers between devices, per_device(): lax.all_gather(query_up_factor, ('req', 'exp'), axis=0, tiled=True)  72.9 us
    all_gather x1, waiting for transfers between devices, per_device(): lax.all_gather(value_down_factor, ('req', 'exp'), axis=0, tiled=True)  59.3 us
    all_gather x1, waiting for transfers between devices, per_device(): lax.all_gather(value_up_factor, ('req', 'exp'), axis=0, tiled=True)  56.6 us
    dot_general x4, matrix products, per_device(): jnp.einsum('jn,nab->jab', selector, piece_in, preferred_element_type=jnp....  18.9 us
    reduce_scatter x1, waiting for transfers between devices, per_device(): lax.psum_scatter(jnp.dot(attended, attention_output_weight, preferred_ele...  17.3 us
  transfers between devices with their start and end apart: 6, of which 6 were waited for; matrix products, arithmetic and copies ran while one was open for 5% of the time, Pallas kernels for 0%

commit v1 on v0

--- a/solution.py
+++ b/solution.py
@@ -9,6 +9,19 @@
 norm_eps = 1e-06
 rope_base = 10000.0
 neg_large = -1e30
+
+
+def collect(x, axis, dim):
+    ways = lax.axis_size(axis)
+    up = [(d, (d + 1) % ways) for d in range(ways)]
+    down = [(d, (d - 1) % ways) for d in range(ways)]
+    earlier, later = ([x], [x])
+    for _ in range(ways // 2):
+        earlier.append(lax.ppermute(earlier[-1], axis, up))
+    for _ in range((ways - 1) // 2):
+        later.append(lax.ppermute(later[-1], axis, down))
+    line = jnp.concatenate([*earlier[::-1], *later[1:]], axis=dim)
+    return jnp.roll(line, (lax.axis_index(axis) - ways // 2) * x.shape[dim], axis=dim)
 
 
 def rms_norm(values, norm_gain):
@@ -154,7 +167,7 @@
     ) + low_rank_term(va_sel, vb_sel, kv_cols, hid_index * kv_cols)
     values_own = values_own.astype(jnp.bfloat16)
     running_max = jnp.full((kv_local, group_share, query_rows), neg_large, jnp.float32)
-    key_piece = lax.all_gather(keys_own, "exp", axis=0, tiled=True)
+    key_piece = collect(keys_own, "exp", 0)
     value_piece = lax.all_gather(values_own, "exp", axis=0, tiled=True)
     piece_len = key_piece.shape[0]
     key_ids = jnp.arange(piece_len, dtype=jnp.int32)

time: 739 us -> 738 us (level)
  blocking collectives: 129 us -> 112 us
  starting transfers between devices: 5.79 us -> 19.5 us
    all_gather x1 -> x0, blocking collectives: 17.2 us -> none  [per_device(): key_piece = lax.all_gather(keys_own, 'exp', axis=0, tiled=True)]
    ppermute x0 -> x7, starting transfers between devices: none -> 13.7 us  [the longest x3 7.47 us: collect(): later.append(lax.ppermute(later[-1], axis, down))]
  transfers between devices with their start and end apart: 6 -> 13, of which waited for: 6 -> 11; matrix products, arithmetic and copies ran while one was open for 5% -> 5% of each run, Pallas kernels for 0% -> 0%
where the time goes in v1:
time: 738 us; the launch traced here: 728 us
  waiting for transfers between devices  451 us (61%)
  blocking collectives  112 us (15%)
  matrix products  57.6 us (8%)
  local copies, waits for them, and re-layouts  43.6 us (6%)
  other arithmetic  29.7 us (4%)
  starting transfers between devices  19.5 us (3%)
  between operations  14.5 us (2%)
    all_to_all x1, waiting for transfers between devices, per_device(): lax.all_to_all(partials, ('exp', 'hid'), split_axis=0, concat_axis=1, til...  163 us
    all_to_all x1, blocking collectives, per_device(): lax.all_to_all(copies, ('exp', 'hid'), split_axis=1, concat_axis=0, tiled...  98.3 us
    all_gather x1, waiting for transfers between devices, per_device(): lax.all_gather(query_down_factor, ('req', 'exp'), axis=0, tiled=True)  76.1 us
    all_gather x1, waiting for transfers between devices, per_device(): lax.all_gather(query_up_factor, ('req', 'exp'), axis=0, tiled=True)  72.9 us
    all_gather x1, waiting for transfers between devices, per_device(): lax.all_gather(value_down_factor, ('req', 'exp'), axis=0, tiled=True)  59.3 us
    all_gather x1, waiting for transfers between devices, per_device(): lax.all_gather(value_up_factor, ('req', 'exp'), axis=0, tiled=True)  56.2 us
    dot_general x4, matrix products, per_device(): jnp.einsum('jn,nab->jab', selector, piece_in, preferred_element_type=jnp....  18.9 us
    reduce_scatter x1, waiting for transfers between devices, per_device(): lax.psum_scatter(jnp.dot(attended, attention_output_weight, preferred_ele...  17.3 us
  transfers between devices with their start and end apart: 13, of which 11 were waited for; matrix products, arithmetic and copies ran while one was open for 5% of the time, Pallas kernels for 0%

profile of v1, /device:TPU:1, one launch (start us, length us, event | category | flops | bytes accessed | tf_op | source)
XLA Modules:
  0.0 727.9 jit_solution(2913210809359474492)
XLA Ops:
  10.1 0.8 reduce-window.10
  11.7 1.4 fusion.19
  13.1 1.7 fusion.82
  15.1 2.7 collective-permute-start
  19.1 2.4 collective-permute-start.1
  22.0 1.9 collective-permute-done.1
  24.0 1.2 collective-permute-start.2
  25.9 3.0 collective-permute-start.5
  29.1 0.7 collective-permute-done.5
  29.8 4.0 collective-permute-start.6
  33.9 0.8 collective-permute-done.6
  34.7 0.8 constant_dynamic-slice_fusion
  35.6 56.2 %all-gather.11.cloned.1.call-done = bf16[64,16,512]{2,1,0:T(8,128)(2,1)} async-done(((bf16[1,16,512]{2,1,0:T(8,128)(2,1)}), bf16[64,16,512]{2,1,0:T(8,128)(2,1)}) %all-gather.11.cloned.1.call-update) | async-done | bytes 1048592 | tf_op jit(solution)/shard_map/all_gather | solution.py:122
  91.8 2.4 fusion.34
  94.3 76.1 %all-gather.5.cloned.1.call-done = bf16[64,1536,16]{1,2,0:T(8,128)(2,1)} async-done(((bf16[1,1536,16]{1,2,0:T(8,128)(2,1)}), bf16[64,1536,16]{1,2,0:T(8,128)(2,1)}) %all-gather.5.cloned.1.call-update) | async-done | bytes 3145744 | tf_op jit(solution)/shard_map/all_gather | solution.py:119
  170.3 5.3 fusion.12
  175.7 72.9 %all-gather.7.cloned.1.call-done = bf16[64,16,1536]{2,1,0:T(8,128)(2,1)} async-done(((bf16[1,16,1536]{2,1,0:T(8,128)(2,1)}), bf16[64,16,1536]{2,1,0:T(8,128)(2,1)}) %all-gather.7.cloned.1.call-update) | async-done | bytes 3145744 | tf_op jit(solution)/shard_map/all_gather | solution.py:120
  248.5 5.4 fusion.8
  254.7 1.4 convolution_add_fusion
  256.1 1.9 copy.89
  258.0 1.1 subtract_convert_fusion
  259.1 7.7 %fusion = (f32[2,3,256]{2,1,0:T(4,128)S(1)}, f32[2,2048,256,3]{2,1,3,0:T(8,128)}) fusion(pred[256,2048]{0,1:T(8,128)(4,1)S(1)} %fusion.18, bf16[2048,2,64,1]{0,2,3,1:T(8,128)(2,1)} %bitcast.141, bf16[256,2,3,32]{0,3,2,1:T(8,128)(2,1)S(1)} %bitcast.147, bf16[256,2,3,32]{0,3,2,1:T(8,128)(2,1)S(1)} %bitcast.146), kind=kOutput, calls=%fused_computation.3 | convolution fusion | flops 412482048 | bytes 13834240 | tf_op jit(solution)/shard_map/qkgh,nkh->kgqn/dot_general | solution.py:179
  267.3 59.3 %all-gather.9.cloned.1.call-done = bf16[64,1536,16]{1,2,0:T(8,128)(2,1)} async-done(((bf16[1,1536,16]{1,2,0:T(8,128)(2,1)}), bf16[64,1536,16]{1,2,0:T(8,128)(2,1)}) %all-gather.9.cloned.1.call-update) | async-done | bytes 3145744 | tf_op jit(solution)/shard_map/all_gather | solution.py:121
  326.6 5.8 fusion.15
  333.6 13.2 %all_gather.19 = bf16[2048,128]{1,0:T(8,128)(2,1)S(1)} all-gather(bf16[256,128]{1,0:T(8,128)(2,1)S(1)} %fusion.33), channel_id=1, replica_groups=mesh['req'=8,'exp'=8,'hid'=4] {'exp'}, dimensions={0}, use_global_device_ids=true | all-gather | bytes 589824 | tf_op jit(solution)/shard_map/all_gather | solution.py:171
  347.0 7.5 %fusion.1 = f32[2,3,256]{2,1,0:T(4,128)S(1)} fusion(f32[2,2048,256,3]{2,1,3,0:T(8,128)} %get-tuple-element.11, f32[2,3,256]{2,1,0:T(4,128)} %broadcast_maximum_fusion, pred[256,2048]{0,1:T(8,128)(4,1)S(1)} %fusion.18), kind=kLoop, calls=%fused_computation.4 | loop fusion | flops 15727104 | bytes 13119488 | tf_op jit(solution)/shard_map/reduce_sum | solution.py:185
  354.5 0.7 copy-done.1
  355.3 3.6 fusion.39
  358.9 1.5 convolution_convert_fusion.1
  360.7 1.2 reduce-window.11
  363.0 17.3 %reduce-scatter.2.cloned.1.call-done = bf16[64,1536]{1,0:T(8,128)(2,1)} async-done(((bf16[256,1536]{1,0:T(8,128)(2,1)}), bf16[64,1536]{1,0:T(8,128)(2,1)}) %reduce-scatter.2.cloned.1.call-update) | async-done | bytes 196624 | tf_op jit(solution)/shard_map/reduce_scatter | solution.py:196
  380.3 1.1 multiply_reduce_fusion.1
  381.5 3.0 convolution_convert_fusion
  384.4 4.3 broadcast_in_dim.129
  388.7 3.2 copy.103
  391.9 1.0 broadcast_in_dim.130
  392.9 98.3 %all_to_all.33 = bf16[16,160,1536]{2,0,1:T(8,128)(2,1)S(1)} all-to-all(bf16[16,160,1536]{2,0,1:T(8,128)(2,1)S(1)} %bitcast.131), channel_id=1, replica_groups=mesh['req'=8,'exp'=8,'hid'=4] {'exp','hid'}, dimensions={1} | all-to-all | bytes 15728640 | tf_op jit(solution)/shard_map/all_to_all | solution.py:229
  491.2 3.9 copy.104
  495.0 6.0 convolution_bitcast_fusion.1
  501.0 12.2 %convert_bitcast_fusion = bf16[512,5,1536]{2,0,1:T(8,128)(2,1)} fusion(bf16[5,128,1536]{2,1,0:T(8,128)(2,1)S(1)} %copy-done, bf16[512,5,1536]{2,0,1:T(8,128)(2,1)} %bitcast.134, bf16[5,1536,128]{2,1,0:T(8,128)(2,1)} %param.36, f32[512,5,128]{2,0,1:T(8,128)S(1)} %convolution_bitcast_fusion.1), kind=kOutput, calls=%fused_computation.6 | convolution fusion | flops 2019164160 | bytes 20971520 | tf_op jit(solution)/shard_map/ref,efd->red/dot_general | solution.py:72
  513.2 12.0 %copy.105 = bf16[512,5,1536]{2,1,0:T(8,128)(2,1)} copy(bf16[512,5,1536]{2,0,1:T(8,128)(2,1)} %convert_bitcast_fusion) | data formatting | bytes 15728640 | tf_op jit(solution)/shard_map/convert_element_type | solution.py:232
  525.1 5.6 all-to-all-start.1
  531.7 162.9 %all-to-all-done.1 = bf16[512,5,1536]{2,1,0:T(8,128)(2,1)} async-done(((bf16[512,5,1536]{2,1,0:T(8,128)(2,1)}), bf16[512,5,1536]{2,1,0:T(8,128)(2,1)}, u32[]{:S(2)}, u32[]{:S(2)}) %all-to-all-start.1) | async-done | bytes 7864352 | tf_op jit(solution)/shard_map/all_to_all | solution.py:233
  694.5 10.2 %reduce.1 = bf16[16,8,5,1536]{3,2,0,1:T(8,128)(2,1)} reduce(bf16[16,8,4,5,1536]{4,3,0,2,1:T(8,128)(2,1)} %bitcast.39, bf16[]{:T(256)} %constant.113.clone.1), dimensions={2}, to_apply=%region_14.15 | reduce | flops 2949120 | bytes 9830402 | tf_op jit(solution)/shard_map/reduce_sum | solution.py:235
  704.7 3.9 copy.107
  708.6 4.3 reshape.289
  712.9 5.4 gather_fusion
  718.3 2.8 multiply_reduce_fusion
  (121 shorter events, 11.8 us)
Async XLA Ops:
  7.2 493.8 %copy-start = (bf16[5,128,1536]{2,1,0:T(8,128)(2,1)S(1)}, bf16[5,128,1536]{2,1,0:T(8,128)(2,1)}, u32[]{:S(2)}) copy-start(bf16[5,128,1536]{2,1,0:T(8,128)(2,1)} %param.37) | copy-start | bytes 5898244
  7.2 18.5 %copy-start.13 = (s32[8,4]{0,1:T(4,128)S(1)}, s32[8,4]{0,1:T(4,128)}, u32[]{:S(2)}) copy-start(s32[8,4]{0,1:T(4,128)} %param.30) | copy-start | bytes 388
  7.2 21.7 %copy-start.21 = (s32[64]{0:T(128)S(1)}, s32[64]{0:T(128)}, u32[]{:S(2)}) copy-start(s32[64]{0:T(128)} %param.31) | copy-start | bytes 772
  7.2 84.6 %all-gather.11.cloned.1.call-start = ((), (), s32[]{:S(2)}) async-start(), calls=%async_computation.6 | async-start | bytes 1064960 | tf_op jit(solution)/shard_map/all_gather | solution.py:122
  7.9 162.4 %all-gather.5.cloned.1.call-start = ((), (), s32[]{:S(2)}) async-start(), calls=%async_computation.3 | async-start | bytes 3194880 | tf_op jit(solution)/shard_map/all_gather | solution.py:119
  8.7 239.9 %all-gather.7.cloned.1.call-start = ((), (), s32[]{:S(2)}) async-start(), calls=%async_computation.4 | async-start | bytes 3194880 | tf_op jit(solution)/shard_map/all_gather | solution.py:120
  9.4 317.2 %all-gather.9.cloned.1.call-start = ((), (), s32[]{:S(2)}) async-start(), calls=%async_computation.5 | async-start | bytes 3194880 | tf_op jit(solution)/shard_map/all_gather | solution.py:121
  10.0 370.3 %reduce-scatter.2.cloned.1.call-start = ((), (), s32[]{:S(2)}) async-start(), calls=%async_computation.7 | async-start | bytes 983040 | tf_op jit(solution)/shard_map/reduce_scatter | solution.py:196
  13.1 8.9 %copy-start.14 = (f32[256]{0:T(256)}, f32[256]{0:T(256)S(1)}, u32[]{:S(2)}) copy-start(f32[256]{0:T(256)S(1)} %add_rsqrt_fusion) | copy-start | bytes 3076
  15.1 4.0 collective-permute-start
  17.8 8.1 %collective-permute-start.4 = (bf16[256,128]{0,1:T(8,128)(2,1)S(1)}, bf16[256,128]{0,1:T(8,128)(2,1)S(1)}, u32[]{:S(2)}, u32[]{:S(2)}) collective-permute-start(bf16[256,128]{0,1:T(8,128)(2,1)S(1)} %bitcast.137), channel_id=1, source_target_pairs={{0,28},{4,0},{8,4},{12,8},{16,12},{20,16},{24,20},{28,24},{1,29},{... | collective-permute-start | bytes 196616 | tf_op jit(solution)/shard_map/ppermute | solution.py:22
  19.1 4.8 collective-permute-start.1
  24.0 4.9 collective-permute-start.2
  25.9 3.9 collective-permute-start.5
  28.9 4.9 collective-permute-start.3
  29.1 141.3 %copy-start.8 = (s32[4]{0:T(128)}, s32[4]{0:T(128)S(1)}, u32[]{:S(2)}) copy-start(s32[4]{0:T(128)S(1)} %select_reduce_fusion.1) | copy-start | bytes 52
  29.8 4.9 collective-permute-start.6
  175.6 78.3 %copy-start.2 = (bf16[256,1536]{1,0:T(8,128)(2,1)S(1)}, bf16[256,1536]{1,0:T(8,128)(2,1)}, u32[]{:S(2)}) copy-start(bf16[256,1536]{1,0:T(8,128)(2,1)} %param.19) | copy-start | bytes 2359300
  248.5 5.4 copy-start.15
  248.5 5.5 copy-start.19
  248.5 5.9 copy-start.10
  248.5 6.1 copy-start.17
  259.1 67.5 %copy-start.9 = (s32[4]{0:T(128)S(1)}, s32[4]{0:T(128)}, u32[]{:S(2)}) copy-start(s32[4]{0:T(128)} %copy-done.8) | copy-start | bytes 52
  266.7 65.7 %copy-start.16 = (f32[256]{0:T(256)S(1)}, f32[256]{0:T(256)}, u32[]{:S(2)}) copy-start(f32[256]{0:T(256)} %copy-done.14) | copy-start | bytes 3076
  266.7 65.7 %copy-start.20 = (f32[1536]{0:T(1024)S(1)}, f32[1536]{0:T(1024)}, u32[]{:S(2)}) copy-start(f32[1536]{0:T(1024)} %param.20) | copy-start | bytes 18436
  267.3 65.6 %copy-start.11 = (pred[256,4]{0,1:T(4,128)(4,1)S(1)}, pred[256,4]{0,1:T(4,128)(4,1)}, u32[]{:S(2)}) copy-start(pred[256,4]{0,1:T(4,128)(4,1)} %iota_compare_fusion.5) | copy-start | bytes 3076
  326.6 6.5 copy-start.18
  347.0 8.2 %copy-start.1 = (f32[2,2048,256,3]{2,1,3,0:T(8,128)S(1)}, f32[2,2048,256,3]{2,1,3,0:T(8,128)}, u32[]{:S(2)}) copy-start(f32[2,2048,256,3]{2,1,3,0:T(8,128)} %get-tuple-element.11) | copy-start | bytes 37748740
  347.0 8.2 %copy-start.5 = (f32[2,3,256]{2,1,0:T(4,128)S(1)}, f32[2,3,256]{2,1,0:T(4,128)}, u32[]{:S(2)}) copy-start(f32[2,3,256]{2,1,0:T(4,128)} %broadcast_maximum_fusion) | copy-start | bytes 18436
  355.3 3.6 copy-start.4
  358.9 1.5 copy-start.6
  358.9 21.5 %copy-start.3 = (bf16[256,1536]{1,0:T(8,128)(2,1)S(1)}, bf16[256,1536]{1,0:T(8,128)(2,1)}, u32[]{:S(2)}) copy-start(bf16[256,1536]{1,0:T(8,128)(2,1)} %param.19) | copy-start | bytes 2359300
  358.9 22.6 %copy-start.7 = (f32[1536]{0:T(1024)S(1)}, f32[1536]{0:T(1024)}, u32[]{:S(2)}) copy-start(f32[1536]{0:T(1024)} %param.32) | copy-start | bytes 18436
  525.1 5.8 copy-start.12
  525.1 169.4 %all-to-all-start.1 = ((bf16[512,5,1536]{2,1,0:T(8,128)(2,1)}), bf16[512,5,1536]{2,1,0:T(8,128)(2,1)}, u32[]{:S(2)}, u32[]{:S(2)}) async-start(bf16[512,5,1536]{2,1,0:T(8,128)(2,1)} %copy.105), calls=%async_computation.2 | async-start | bytes 25165824 | tf_op jit(solution)/shard_map/all_to_all | solution.py:233
Sparse Core Ops, SparseCore 0:
  10.8 80.9 all-gather.10
  94.6 75.7 all-gather.4
  173.1 75.4 all-gather.6
  251.2 75.4 all-gather.8
  360.5 19.7 reduce-scatter.1
